TPU v7x, 128 devices: a whole 4x4x4 slice. The times are simulated.
128 devices in a mesh: wide: 16 (over z, y), col: 8 (over x, core).
Axes of the slice: x: 4, y: 4, z: 4, core: 2. Of those that a mesh axis runs over, the one named last changes fastest.
Arguments:
- z_root: float32 [512, 16384], P('col', 'wide'), may hold values from -6 to 6
- z_child: float32 [512, 2, 8192], P('col', None, 'wide'), may hold values from -6 to 6
- z_grand: float32 [512, 4, 4096], P('col', None, 'wide'), may hold values from -6 to 6
- inv_root: float32 [16384, 16384], P('wide', 'col'), as said below
- inv_child: float32 [2, 8192, 8192], P(None, 'wide', 'col'), as said below
- inv_grand: float32 [4, 4096, 4096], P(None, 'wide', 'col'), as said below
- panel_child: float32 [2, 4096, 8192], P(None, 'col', 'wide'), may hold values from -0.046875 to 0.046875
- panel_grand: float32 [4, 2048, 4096], P(None, 'col', 'wide'), may hold values from -0.0625 to 0.0625
- anc_child: int32 [2, 32], P(None, 'col'), may hold values from 0 to 127, as said below
- anc_grand: int32 [4, 16], P(None, 'col'), may hold values from 0 to 255, as said below
Outputs:
- x_root: float32 [512, 16384], P('wide', 'col')
- x_child: float32 [512, 2, 8192], P('wide', None, 'col')
- x_grand: float32 [512, 4, 4096], P('wide', None, 'col')
Inputs may be any that keep to these rules, and one draw needn't show every extreme that they name: inv_root is lower triangular with a positive diagonal (entries above the diagonal are zero). Each inv_child[k] is lower triangular with a positive diagonal. Each inv_grand[g] is lower triangular with a positive diagonal. `anc_child`: each row lists distinct blocks in rising order and always names block 0 and block 127. `anc_grand`: row g lists 2048 // 256 distinct root blocks in rising order, block 0 and block 127 among them, then as many distinct blocks of child g // 2 (numbered 16384 // 128 + (g // 2) * 64 onwards) in rising order, its first and its last among them.
All inputs are finite; a program needn't handle non-finite values.
Results may differ from a plain program's by a relative error of at most 0.000096.
Values sent between devices are 32-bit elements; how exact they have to be, the bound alone decides.
No kernel may reach another device: no remote copies, remote signals or barrier semaphores. Data moves between devices by JAX's collectives and lax.ppermute only.
A program may use at most 128 MiB of HBM per device.

v0:
```python
import jax
import jax.numpy as jnp
from jax import lax
from jax.sharding import PartitionSpec as P

BLK = 128
PRECISE = lax.Precision.HIGHEST


def pick_blocks(source_rows, blocks):
    leading = source_rows.shape[0]
    tiled = source_rows.reshape(leading, source_rows.shape[1] // BLK, BLK)
    selected = jnp.take(tiled, blocks.reshape(-1), axis=1)
    return selected.reshape(leading, blocks.shape[0], blocks.shape[1] * BLK)


def spread_rhs(local_part):
    return lax.all_gather(local_part, "col", axis=0, tiled=True)


def solve_terms(right_rows, inverse):
    return lax.psum_scatter(
        jnp.einsum(
            "ski,kij->skj",
            right_rows,
            inverse,
            precision=PRECISE,
            preferred_element_type=jnp.float32,
        ),
        "wide",
        scatter_dimension=0,
        tiled=True,
    )


def spread_solved(solved_local):
    gathered = lax.all_gather(solved_local, "col", axis=2, tiled=True)
    return gathered.reshape(gathered.shape[0], -1)


def fetch_ancestors(source_rows, blocks):
    return lax.all_gather(pick_blocks(source_rows, blocks), "wide", axis=0, tiled=True)


def finish_level(z_local, inverse, partial_value):
    summed = lax.psum(partial_value, "col")
    right_side = spread_rhs(z_local) - summed
    solved = solve_terms(right_side, inverse)
    return solved


def per_device(
    z_root,
    z_child,
    z_grand,
    inv_root,
    inv_child,
    inv_grand,
    panel_child,
    panel_grand,
    anc_child,
    anc_grand,
):
    root_right = spread_rhs(z_root[:, None, :])
    root_solved = solve_terms(root_right, inv_root[None])
    x_root = root_solved[:, 0, :]
    root_rows = spread_solved(root_solved)
    near_rows = fetch_ancestors(root_rows, anc_child)
    partial_value = jnp.einsum(
        "ska,kaj->skj",
        near_rows,
        panel_child,
        precision=PRECISE,
        preferred_element_type=jnp.float32,
    )
    x_child = finish_level(z_child, inv_child, partial_value)
    child_rows = spread_solved(x_child)
    solved_all = jnp.concatenate([root_rows, child_rows], axis=1)
    far_rows = fetch_ancestors(solved_all, anc_grand)
    partial_grand = jnp.einsum(
        "sga,gaj->sgj", far_rows, panel_grand, precision=PRECISE, preferred_element_type=jnp.float32
    )
    x_grand = finish_level(z_grand, inv_grand, partial_grand)
    return (x_root, x_child, x_grand)


def solution(mesh):
    in_specs = (
        P("col", "wide"),
        P("col", None, "wide"),
        P("col", None, "wide"),
        P("wide", "col"),
        P(None, "wide", "col"),
        P(None, "wide", "col"),
        P(None, "col", "wide"),
        P(None, "col", "wide"),
        P(None, "col"),
        P(None, "col"),
    )
    out_specs = (P("wide", "col"), P("wide", None, "col"), P("wide", None, "col"))
    return jax.shard_map(
        per_device, mesh=mesh, in_specs=in_specs, out_specs=out_specs, check_vma=False
    )
```

profile of v0, /device:TPU:0, one launch (start us, length us, event | category | flops | bytes accessed | tf_op | source)
XLA Modules:
  0.0 726.2 jit_solution(2255232434404925078)
XLA Ops:
  7.2 0.0 all-gather.21.cloned.1.call-start
  7.2 0.7 all-gather.21.cloned.1.call-update
  7.9 0.0 all-reduce.9.cloned.1.call-start
  8.0 29.4 %all-gather.21.cloned.1.call-done = f32[512,1024]{1,0:T(8,128)} async-done(((f32[64,1024]{1,0:T(8,128)}), f32[512,1024]{1,0:T(8,128)}) %all-gather.21.cloned.1.call-update) | async-done | bytes 2097168 | tf_op jit(solution)/shard_map/all_gather | solution.py:18
  37.4 30.4 %convolution_bitcast_fusion = f32[512,1,2048]{0,2,1:T(8,128)} fusion(f32[1024,2048]{1,0:T(8,128)} %param.13, f32[512,1024]{1,0:T(8,128)} %all-gather.21.cloned.1.call-done), kind=kOutput, calls=%fused_computation.3 | convolution fusion | flops 12884901888 | bytes 14680064 | tf_op jit(solution)/shard_map/ski,kij->skj/dot_general | solution.py:23
  67.8 11.0 %copy.75 = f32[512,1,2048]{2,1,0:T(1,128)} copy(f32[512,1,2048]{0,2,1:T(8,128)} %convolution_bitcast_fusion) | data formatting | bytes 8388608 | tf_op jit(solution)/shard_map/ski,kij->skj/transpose | solution.py:23
  78.8 0.0 all-reduce.9.cloned.1.call-update
  78.8 0.0 all-gather.11.cloned.1.call-start
  78.9 0.6 copy-done.8
  79.5 0.6 dynamic-slice
  80.7 102.2 %all-reduce.9.cloned.1.call-done = f32[512,1,2048]{2,1,0:T(1,128)} async-done(((f32[512,1,2048]{2,1,0:T(1,128)}), f32[512,1,2048]{2,1,0:T(1,128)}) %all-reduce.9.cloned.1.call-update) | async-done | bytes 4194320
  183.0 1.7 constant_dynamic-slice_fusion
  184.6 0.0 all-gather.11.cloned.1.call-update
  184.7 0.0 all-gather.13.cloned.1.call-start
  184.7 0.1 reshape.104
  184.8 0.1 broadcast_bitcast_fusion.1
  184.9 25.1 %all-gather.11.cloned.1.call-done = f32[32,1,16384]{2,1,0:T(1,128)} async-done(((f32[32,1,2048]{2,1,0:T(1,128)}), f32[32,1,16384]{2,1,0:T(1,128)}) %all-gather.11.cloned.1.call-update) | async-done | bytes 2097168 | tf_op jit(solution)/shard_map/all_gather | solution.py:37
  210.0 4.2 copy.77
  214.3 2.1 gather_fusion
  216.4 0.1 copy.78
  216.5 0.1 gather.13
  216.6 0.7 copy_select_fusion.1
  217.3 0.0 all-gather.13.cloned.1.call-update
  217.3 0.0 all-gather.9.cloned.1.call-start
  217.3 0.8 copy.76
  218.1 0.0 all-gather.9.cloned.1.call-update
  218.1 0.0 all-reduce.5.cloned.1.call-start
  218.2 44.9 %all-gather.13.cloned.1.call-done = f32[512,2,512]{2,0,1:T(8,128)} async-done(((f32[32,2,512]{2,0,1:T(8,128)}), f32[512,2,512]{2,0,1:T(8,128)}) %all-gather.13.cloned.1.call-update) | async-done | bytes 2097168 | tf_op jit(solution)/shard_map/all_gather | solution.py:42
  263.0 7.0 convolution_bitcast_fusion.4
  270.1 0.0 all-reduce.5.cloned.1.call-update
  270.1 0.0 reduce-scatter.3.cloned.1.call-start
  270.1 19.4 %all-gather.9.cloned.1.call-done = f32[512,2,512]{2,0,1:T(8,128)} async-done(((f32[64,2,512]{2,0,1:T(8,128)}), f32[512,2,512]{2,0,1:T(8,128)}) %all-gather.9.cloned.1.call-update) | async-done | bytes 2097168 | tf_op jit(solution)/shard_map/all_gather | solution.py:18
  289.6 68.2 %all-reduce.5.cloned.1.call-done = f32[512,2,512]{2,0,1:T(8,128)} async-done(((f32[512,2,512]{2,0,1:T(8,128)}), f32[512,2,512]{2,0,1:T(8,128)}) %all-reduce.5.cloned.1.call-update) | async-done | bytes 2097168 | tf_op jit(solution)/shard_map/psum | solution.py:46
  357.8 12.2 %convolution_bitcast_fusion.2 = f32[512,2,1024]{2,0,1:T(8,128)} fusion(f32[2,512,1024]{2,1,0:T(8,128)} %param.14, f32[512,2,512]{2,0,1:T(8,128)} %all-gather.9.cloned.1.call-done, f32[512,2,512]{2,0,1:T(8,128)} %all-reduce.5.cloned.1.call-done), kind=kOutput, calls=%fused_computation.5 | convolution fusion | flops 6442975232 | bytes 12582912 | tf_op jit(solution)/shard_map/ski,kij->skj/dot_general | solution.py:23
  370.0 0.0 reduce-scatter.3.cloned.1.call-update
  370.0 0.0 all-gather.17.cloned.1.call-start
  370.1 77.5 %reduce-scatter.3.cloned.1.call-done = f32[32,2,1024]{2,0,1:T(8,128)} async-done(((f32[512,2,1024]{2,0,1:T(8,128)}), f32[32,2,1024]{2,0,1:T(8,128)}) %reduce-scatter.3.cloned.1.call-update) | async-done | bytes 262160 | tf_op jit(solution)/shard_map/reduce_scatter | solution.py:22
  447.6 0.0 all-gather.19.cloned.1.call-start
  447.6 0.1 copy.84
  447.7 0.1 reshape.105
  447.9 0.1 broadcast_bitcast_fusion
  447.9 25.8 %all-gather.17.cloned.1.call-done = f32[32,2,8192]{2,0,1:T(8,128)} async-done(((f32[32,2,1024]{2,0,1:T(8,128)}), f32[32,2,8192]{2,0,1:T(8,128)}) %all-gather.17.cloned.1.call-update) | async-done | bytes 2097168 | tf_op jit(solution)/shard_map/all_gather | solution.py:37
  473.7 4.6 copy.81
  478.3 4.0 concatenate.6
  482.3 3.0 copy.83
  485.3 2.4 pad_maximum_fusion
  487.7 2.8 gather_fusion.1
  490.5 0.1 copy.85
  490.6 0.1 gather.15
  490.7 0.7 copy_select_fusion
  491.4 0.0 all-gather.15.cloned.1.call-start
  491.4 1.7 copy.80
  493.2 0.0 all-reduce.7.cloned.1.call-start
  493.2 43.9 %all-gather.19.cloned.1.call-done = f32[512,4,256]{2,0,1:T(8,128)} async-done(((f32[32,4,256]{2,0,1:T(8,128)}), f32[512,4,256]{2,0,1:T(8,128)}) %all-gather.19.cloned.1.call-update) | async-done | bytes 2097168 | tf_op jit(solution)/shard_map/all_gather | solution.py:42
  537.1 4.9 convolution_bitcast_fusion.3
  542.0 0.0 reduce-scatter.5.cloned.1.call-start
  542.1 21.7 %all-gather.15.cloned.1.call-done = f32[512,4,256]{2,0,1:T(8,128)} async-done(((f32[64,4,256]{2,0,1:T(8,128)}), f32[512,4,256]{2,0,1:T(8,128)}) %all-gather.15.cloned.1.call-update) | async-done | bytes 2097168 | tf_op jit(solution)/shard_map/all_gather | solution.py:18
  563.8 68.5 %all-reduce.7.cloned.1.call-done = f32[512,4,256]{2,0,1:T(8,128)} async-done(((f32[512,4,256]{2,0,1:T(8,128)}), f32[512,4,256]{2,0,1:T(8,128)}) %all-reduce.7.cloned.1.call-update) | async-done | bytes 2097168 | tf_op jit(solution)/shard_map/psum | solution.py:46
  632.3 7.8 %convolution_bitcast_fusion.1 = f32[512,4,512]{2,0,1:T(8,128)} fusion(f32[4,256,512]{2,1,0:T(8,128)S(1)} %copy-done, f32[512,4,256]{2,0,1:T(8,128)} %all-gather.15.cloned.1.call-done, f32[512,4,256]{2,0,1:T(8,128)} %all-reduce.7.cloned.1.call-done), kind=kOutput, calls=%fused_computation.4 | convolution fusion | flops 3221749760 | bytes 10485760 | tf_op jit(solution)/shard_map/ski,kij->skj/dot_general | solution.py:23
  640.0 0.9 copy-done.2
  641.0 0.8 copy.95
  641.8 0.9 copy.87
  642.7 74.9 %reduce-scatter.5.cloned.1.call-done = f32[32,4,512]{2,0,1:T(8,128)} async-done(((f32[512,4,512]{2,0,1:T(8,128)}), f32[32,4,512]{2,0,1:T(8,128)}) %reduce-scatter.5.cloned.1.call-update) | async-done | bytes 262160 | tf_op jit(solution)/shard_map/reduce_scatter | solution.py:22
  717.6 1.8 copy.88
  (28 shorter events, 0.2 us)
Async XLA Ops:
  7.2 625.1 %copy-start = (f32[4,256,512]{2,1,0:T(8,128)S(1)}, f32[4,256,512]{2,1,0:T(8,128)}, u32[]{:S(2)}) copy-start(f32[4,256,512]{2,1,0:T(8,128)} %param.15) | copy-start | bytes 6291460
  7.2 30.2 %all-gather.21.cloned.1.call-start = ((), (), s32[]{:S(2)}) async-start(), calls=%async_computation.12 | async-start | bytes 2359296 | tf_op jit(solution)/shard_map/all_gather | solution.py:18
  7.9 175.0 %all-reduce.9.cloned.1.call-start = ((), (), s32[]{:S(2)}) async-start(), calls=%async_computation.13 | async-start | bytes 8388608
  78.8 0.7 copy-start.8
  78.8 105.9 %copy-start.7 = (s32[2,4]{1,0:T(2,128)S(1)}, s32[2,4]{1,0:T(2,128)}, u32[]{:S(2)}) copy-start(s32[2,4]{1,0:T(2,128)} %param.18) | copy-start | bytes 100
  78.8 131.2 %all-gather.11.cloned.1.call-start = ((), (), s32[]{:S(2)}) async-start(), calls=%async_computation.3 | async-start | bytes 2359296 | tf_op jit(solution)/shard_map/all_gather | solution.py:37
  184.7 78.4 %all-gather.13.cloned.1.call-start = ((), (), s32[]{:S(2)}) async-start(), calls=%async_computation.4 | async-start | bytes 2228224 | tf_op jit(solution)/shard_map/all_gather | solution.py:42
  210.0 7.3 %copy-start.5 = (f32[64,2,512]{2,1,0:T(2,128)S(1)}, f32[64,2,512]{2,1,0:T(2,128)}, u32[]{:S(2)}) copy-start(f32[64,2,512]{2,1,0:T(2,128)} %param.11) | copy-start | bytes 786436
  217.3 72.3 %all-gather.9.cloned.1.call-start = ((), (), s32[]{:S(2)}) async-start(), calls=%async_computation.2 | async-start | bytes 2359296 | tf_op jit(solution)/shard_map/all_gather | solution.py:18
  218.1 139.7 %all-reduce.5.cloned.1.call-start = ((), (), s32[]{:S(2)}) async-start(), calls=%async_computation.5 | async-start | bytes 4194304 | tf_op jit(solution)/shard_map/psum | solution.py:46
  270.1 177.5 %reduce-scatter.3.cloned.1.call-start = ((), (), s32[]{:S(2)}) async-start(), calls=%async_computation.6 | async-start | bytes 4456448 | tf_op jit(solution)/shard_map/reduce_scatter | solution.py:22
  370.0 77.7 %copy-start.6 = (s32[4,2]{0,1:T(2,128)S(1)}, s32[4,2]{0,1:T(2,128)}, u32[]{:S(2)}) copy-start(s32[4,2]{0,1:T(2,128)} %param.19) | copy-start | bytes 100
  370.0 103.7 %all-gather.17.cloned.1.call-start = ((), (), s32[]{:S(2)}) async-start(), calls=%async_computation.8 | async-start | bytes 2359296 | tf_op jit(solution)/shard_map/all_gather | solution.py:37
  447.6 89.6 %all-gather.19.cloned.1.call-start = ((), (), s32[]{:S(2)}) async-start(), calls=%async_computation.9 | async-start | bytes 2228224 | tf_op jit(solution)/shard_map/all_gather | solution.py:42
  482.3 3.0 copy-start.1
  487.7 49.5 %copy-start.3 = (f32[4,256,256]{2,1,0:T(8,128)S(1)}, f32[4,256,256]{2,1,0:T(8,128)}, u32[]{:S(2)}) copy-start(f32[4,256,256]{2,1,0:T(8,128)} %param.17) | copy-start | bytes 3145732
  491.4 72.4 %all-gather.15.cloned.1.call-start = ((), (), s32[]{:S(2)}) async-start(), calls=%async_computation.7 | async-start | bytes 2359296 | tf_op jit(solution)/shard_map/all_gather | solution.py:18
  493.2 139.1 %all-reduce.7.cloned.1.call-start = ((), (), s32[]{:S(2)}) async-start(), calls=%async_computation.10 | async-start | bytes 4194304 | tf_op jit(solution)/shard_map/psum | solution.py:46
  542.0 175.5 %reduce-scatter.5.cloned.1.call-start = ((), (), s32[]{:S(2)}) async-start(), calls=%async_computation.11 | async-start | bytes 4456448 | tf_op jit(solution)/shard_map/reduce_scatter | solution.py:22
  640.0 0.9 copy-start.2
  640.0 1.7 copy-start.4
Sparse Core Ops, SparseCore 0:
  9.7 27.5 all-gather.20
  79.0 103.9 all-reduce.8
  185.2 24.7 all-gather.10
  217.4 45.5 all-gather.12
  265.2 24.3 all-gather.8
  291.8 65.9 all-reduce.4
  370.1 77.3 reduce-scatter.2
  449.4 24.3 all-gather.16
  491.5 45.5 all-gather.18
  539.4 24.3 all-gather.14
  566.3 65.9 all-reduce.6
  640.2 77.3 reduce-scatter.4
where the time goes:
time: 727 us; the launch traced here: 726 us
  waiting for transfers between devices  602 us (83%)
  matrix products  62.3 us (9%)
  local copies, waits for them, and re-layouts  42.2 us (6%)
  between operations  15 us (2%)
    reduce_scatter x2, waiting for transfers between devices, solve_terms(): lax.psum_scatter(jnp.einsum('ski,kij->skj', right_rows, inverse, precisio...  152 us
    psum x2, waiting for transfers between devices, finish_level(): summed = lax.psum(partial_value, 'col')  137 us
    unnamed x13, waiting for transfers between devices  103 us
    all_gather x2, waiting for transfers between devices, fetch_ancestors(): lax.all_gather(pick_blocks(source_rows, blocks), 'wide', axis=0, tiled=True)  88.8 us
    all_gather x3, waiting for transfers between devices, spread_rhs(): return lax.all_gather(local_part, 'col', axis=0, tiled=True)  70.5 us
    all_gather x2, waiting for transfers between devices, spread_solved(): gathered = lax.all_gather(solved_local, 'col', axis=2, tiled=True)  50.9 us
    dot_general x3, matrix products, solve_terms(): jnp.einsum('ski,kij->skj', right_rows, inverse, precision=PRECISE, prefer...  50.4 us
  transfers between devices with their start and end apart: 12, of which 12 were waited for; matrix products, arithmetic and copies ran while one was open for 2% of the time, Pallas kernels for 0%

commit v1 on v0

--- a/solution.py
+++ b/solution.py
@@ -5,6 +5,24 @@
 
 BLK = 128
 PRECISE = lax.Precision.HIGHEST
+
+
+def ring_gather(value, axis, dim):
+    ways, here, step = (lax.axis_size(axis), lax.axis_index(axis), value.shape[dim])
+    shape = [n * ways if d == dim else n for d, n in enumerate(value.shape)]
+    full = lax.dynamic_update_slice_in_dim(
+        jnp.zeros(shape, value.dtype), value, here * step, axis=dim
+    )
+    going_up = going_down = value
+    for far in range(1, ways // 2 + 1):
+        going_up = lax.ppermute(going_up, axis, [(d, (d + 1) % ways) for d in range(ways)])
+        full = lax.dynamic_update_slice_in_dim(full, going_up, (here - far) % ways * step, axis=dim)
+        if 2 * far < ways:
+            going_down = lax.ppermute(going_down, axis, [(d, (d - 1) % ways) for d in range(ways)])
+            full = lax.dynamic_update_slice_in_dim(
+                full, going_down, (here + far) % ways * step, axis=dim
+            )
+    return full
 
 
 def pick_blocks(source_rows, blocks):
@@ -15,7 +33,7 @@
 
 
 def spread_rhs(local_part):
-    return lax.all_gather(local_part, "col", axis=0, tiled=True)
+    return ring_gather(local_part, "col", 0)
 
 
 def solve_terms(right_rows, inverse):

time: 727 us -> 630 us (0.87)
  waiting for transfers between devices: 602 us -> 495 us
  starting transfers between devices: 0.49 us -> 23.9 us
  matrix products: 62.3 us -> 49.4 us
    unnamed x13 -> x9, waiting for transfers between devices: 103 us -> 0.15 us
    reduce_scatter x2 -> x3, waiting for transfers between devices: 152 us -> 231 us  [solve_terms(): lax.psum_scatter(jnp.einsum('ski,kij->skj', right_rows, inverse, precisio...]
    all_gather x3 -> x0, waiting for transfers between devices: 70.5 us -> none  [spread_rhs(): return lax.all_gather(local_part, 'col', axis=0, tiled=True)]
    ppermute x0 -> x21, waiting for transfers between devices: none -> 41.9 us  [the longest x12 35.2 us: ring_gather(): lax.ppermute(going_up, axis, [(d, (d + 1) % ways) for d in range(ways)])]
    psum x2, waiting for transfers between devices: 137 us -> 98.2 us  [finish_level(): summed = lax.psum(partial_value, 'col')]
    ppermute x0 -> x21, starting transfers between devices: none -> 23.1 us  [the longest x9 22.6 us: ring_gather(): lax.ppermute(going_down, axis, [(d, (d - 1) % ways) for d in range(ways)])]
    all_gather x2, waiting for transfers between devices: 88.8 us -> 72.1 us  [fetch_ancestors(): lax.all_gather(pick_blocks(source_rows, blocks), 'wide', axis=0, tiled=True)]
    dot_general x3, matrix products: 50.4 us -> 37.4 us  [solve_terms(): jnp.einsum('ski,kij->skj', right_rows, inverse, precision=PRECISE, prefer...]
  transfers between devices with their start and end apart: 12 -> 30, of which waited for: 12 -> 21; matrix products, arithmetic and copies ran while one was open for 2% -> 5% of each run, Pallas kernels for 0% -> 0%
where the time goes in v1:
time: 630 us; the launch traced here: 629 us
  waiting for transfers between devices  495 us (79%)
  matrix products  49.4 us (8%)
  local copies, waits for them, and re-layouts  42.8 us (7%)
  starting transfers between devices  23.9 us (4%)
  between operations  14.1 us (2%)
    reduce_scatter x3, waiting for transfers between devices, solve_terms(): lax.psum_scatter(jnp.einsum('ski,kij->skj', right_rows, inverse, precisio...  231 us
    psum x2, waiting for transfers between devices, finish_level(): summed = lax.psum(partial_value, 'col')  98.2 us
    all_gather x2, waiting for transfers between devices, fetch_ancestors(): lax.all_gather(pick_blocks(source_rows, blocks), 'wide', axis=0, tiled=True)  72.1 us
    all_gather x2, waiting for transfers between devices, spread_solved(): gathered = lax.all_gather(solved_local, 'col', axis=2, tiled=True)  51.8 us
    dot_general x3, matrix products, solve_terms(): jnp.einsum('ski,kij->skj', right_rows, inverse, precision=PRECISE, prefer...  37.4 us
    ppermute x12, waiting for transfers between devices, ring_gather(): lax.ppermute(going_up, axis, [(d, (d + 1) % ways) for d in range(ways)])  35.2 us
    ppermute x9, starting transfers between devices, ring_gather(): lax.ppermute(going_down, axis, [(d, (d - 1) % ways) for d in range(ways)])  22.6 us
  transfers between devices with their start and end apart: 30, of which 21 were waited for; matrix products, arithmetic and copies ran while one was open for 5% of the time, Pallas kernels for 0%

profile of v1, /device:TPU:0, one launch (start us, length us, event | category | flops | bytes accessed | tf_op | source)
XLA Modules:
  0.0 629.2 jit_solution(11453861854139410501)
XLA Ops:
  7.3 2.9 collective-permute-start.1
  10.5 4.0 collective-permute-done
  14.5 3.0 collective-permute-start.3
  17.5 4.0 collective-permute-done.2
  21.5 3.0 collective-permute-start.5
  24.5 4.0 collective-permute-done.4
  28.6 6.9 %collective-permute-done.6 = f32[64,1,1024]{2,0,1:T(8,128)S(1)} collective-permute-done((f32[64,1,1024]{2,0,1:T(8,128)S(1)}, f32[64,1,1024]{2,0,1:T(8,128)S(1)}, u32[]{:S(2)}, u32[]{:S(2)}) %collective-permute-start.6) | collective-permute-done | bytes 262176 | tf_op jit(solution)/shard_map/ppermute | solution.py:18
  35.5 17.4 %convolution_bitcast_fusion = f32[512,1,2048]{2,0,1:T(8,128)} fusion(f32[512,1024]{1,0:T(8,128)S(1)} %bitcast_dynamic-update-slice_fusion, f32[1024,2048]{1,0:T(8,128)} %param.13), kind=kOutput, calls=%fused_computation.3 | convolution fusion | flops 12884901888 | bytes 14680064 | tf_op jit(solution)/shard_map/ski,kij->skj/dot_general | solution.py:41
  53.0 77.9 %reduce-scatter.4.cloned.1.call-done = f32[32,1,2048]{2,0,1:T(8,128)} async-done(((f32[512,1,2048]{2,0,1:T(8,128)}), f32[32,1,2048]{2,0,1:T(8,128)}) %reduce-scatter.4.cloned.1.call-update) | async-done | bytes 262160 | tf_op jit(solution)/shard_map/reduce_scatter | solution.py:40
  131.3 26.3 %all-gather.5.cloned.1.call-done = f32[32,1,16384]{2,0,1:T(8,128)} async-done(((f32[32,1,2048]{2,0,1:T(8,128)}), f32[32,1,16384]{2,0,1:T(8,128)}) %all-gather.5.cloned.1.call-update) | async-done | bytes 2097168 | tf_op jit(solution)/shard_map/all_gather | solution.py:55
  157.7 2.0 copy.74
  159.6 2.6 copy.59
  162.2 2.2 gather_fusion
  165.5 1.6 broadcast_in_dim.40
  167.1 0.8 fusion.5
  168.2 2.7 collective-permute-start.8
  170.9 4.1 collective-permute-done.7
  174.9 36.1 %all-gather.7.cloned.1.call-done = f32[512,2,512]{2,0,1:T(8,128)} async-done(((f32[32,2,512]{2,0,1:T(8,128)}), f32[512,2,512]{2,0,1:T(8,128)}) %all-gather.7.cloned.1.call-update) | async-done | bytes 2097168 | tf_op jit(solution)/shard_map/all_gather | solution.py:60
  211.1 7.1 %convolution_bitcast_fusion.4 = f32[512,2,512]{2,0,1:T(8,128)} fusion(f32[512,2,512]{2,0,1:T(8,128)} %all-gather.7.cloned.1.call-done, f32[2,512,512]{2,1,0:T(8,128)} %param.16), kind=kOutput, calls=%fused_computation.9 | convolution fusion | flops 3221225472 | bytes 6291456 | tf_op jit(solution)/shard_map/ska,kaj->skj/dot_general | solution.py:87
  218.2 1.1 collective-permute-start.10
  219.3 0.7 constant_dynamic-update-slice_fusion.14
  220.1 0.7 constant_dynamic-update-slice_fusion.13
  220.8 2.4 collective-permute-done.10
  223.2 3.1 collective-permute-start.12
  226.3 0.7 constant_dynamic-update-slice_fusion.12
  227.0 0.7 constant_dynamic-update-slice_fusion.11
  227.8 0.7 constant_dynamic-update-slice_fusion.10
  228.5 1.7 collective-permute-done.12
  230.2 0.7 constant_dynamic-update-slice_fusion.9
  230.9 4.1 collective-permute-done.13
  235.0 0.7 constant_dynamic-update-slice_fusion.8
  235.7 49.0 %all-reduce.3.cloned.1.call-done = f32[512,2,512]{2,0,1:T(8,128)} async-done(((f32[512,2,512]{2,0,1:T(8,128)}), f32[512,2,512]{2,0,1:T(8,128)}) %all-reduce.3.cloned.1.call-update) | async-done | bytes 2097168 | tf_op jit(solution)/shard_map/psum | solution.py:64
  284.8 12.2 %convolution_bitcast_fusion.2 = f32[512,2,1024]{2,0,1:T(8,128)} fusion(f32[2,512,1024]{2,1,0:T(8,128)} %param.14, f32[512,2,512]{2,0,1:T(8,128)} %constant_dynamic-update-slice_fusion.8, f32[512,2,512]{2,0,1:T(8,128)} %all-reduce.3.cloned.1.call-done), kind=kOutput, calls=%fused_computation.5 | convolution fusion | flops 6442975232 | bytes 12582912 | tf_op jit(solution)/shard_map/ski,kij->skj/dot_general | solution.py:41
  297.1 77.5 %reduce-scatter.6.cloned.1.call-done = f32[32,2,1024]{2,0,1:T(8,128)} async-done(((f32[512,2,1024]{2,0,1:T(8,128)}), f32[32,2,1024]{2,0,1:T(8,128)}) %reduce-scatter.6.cloned.1.call-update) | async-done | bytes 262160 | tf_op jit(solution)/shard_map/reduce_scatter | solution.py:40
  374.9 25.5 %all-gather.9.cloned.1.call-done = f32[32,2,8192]{2,0,1:T(8,128)} async-done(((f32[32,2,1024]{2,0,1:T(8,128)}), f32[32,2,8192]{2,0,1:T(8,128)}) %all-gather.9.cloned.1.call-update) | async-done | bytes 2097168 | tf_op jit(solution)/shard_map/all_gather | solution.py:55
  400.4 4.6 copy.65
  405.0 4.0 concatenate.6
  409.0 3.0 copy.67
  412.0 2.4 pad_maximum_fusion
  414.4 2.8 gather_fusion.1
  418.2 1.6 broadcast_in_dim.45
  419.8 0.9 fusion.4
  420.9 2.7 collective-permute-start.15
  423.6 4.4 collective-permute-done.14
  427.9 36.0 %all-gather.11.cloned.1.call-done = f32[512,4,256]{2,0,1:T(8,128)} async-done(((f32[32,4,256]{2,0,1:T(8,128)}), f32[512,4,256]{2,0,1:T(8,128)}) %all-gather.11.cloned.1.call-update) | async-done | bytes 2097168 | tf_op jit(solution)/shard_map/all_gather | solution.py:60
  463.9 4.9 convolution_bitcast_fusion.3
  468.9 1.1 collective-permute-start.17
  470.0 1.7 constant_dynamic-update-slice_fusion.6
  471.7 1.7 constant_dynamic-update-slice_fusion.5
  473.3 0.9 collective-permute-done.17
  474.2 3.0 collective-permute-start.19
  477.2 0.7 constant_dynamic-update-slice_fusion.4
  477.9 0.7 constant_dynamic-update-slice_fusion.3
  478.7 0.7 constant_dynamic-update-slice_fusion.2
  479.4 1.7 collective-permute-done.19
  481.1 0.7 constant_dynamic-update-slice_fusion.1
  481.8 3.8 collective-permute-done.20
  485.6 0.7 constant_dynamic-update-slice_fusion
  486.4 49.1 %all-reduce.5.cloned.1.call-done = f32[512,4,256]{2,0,1:T(8,128)} async-done(((f32[512,4,256]{2,0,1:T(8,128)}), f32[512,4,256]{2,0,1:T(8,128)}) %all-reduce.5.cloned.1.call-update) | async-done | bytes 2097168 | tf_op jit(solution)/shard_map/psum | solution.py:64
  535.5 7.8 %convolution_bitcast_fusion.1 = f32[512,4,512]{2,0,1:T(8,128)} fusion(f32[4,256,512]{2,1,0:T(8,128)S(1)} %copy-done, f32[512,4,256]{2,0,1:T(8,128)} %constant_dynamic-update-slice_fusion, f32[512,4,256]{2,0,1:T(8,128)} %all-reduce.5.cloned.1.call-done), kind=kOutput, calls=%fused_computation.4 | convolution fusion | flops 3221749760 | bytes 10485760 | tf_op jit(solution)/shard_map/ski,kij->skj/dot_general | solution.py:41
  543.3 0.9 copy-done.3
  544.2 0.9 copy.71
  545.1 75.8 %reduce-scatter.8.cloned.1.call-done = f32[32,4,512]{2,0,1:T(8,128)} async-done(((f32[512,4,512]{2,0,1:T(8,128)}), f32[32,4,512]{2,0,1:T(8,128)}) %reduce-scatter.8.cloned.1.call-update) | async-done | bytes 262160 | tf_op jit(solution)/shard_map/reduce_scatter | solution.py:40
  620.9 1.8 copy.72
  (82 shorter events, 4.1 us)
Async XLA Ops:
  7.2 528.3 %copy-start = (f32[4,256,512]{2,1,0:T(8,128)S(1)}, f32[4,256,512]{2,1,0:T(8,128)}, u32[]{:S(2)}) copy-start(f32[4,256,512]{2,1,0:T(8,128)} %param.15) | copy-start | bytes 6291460
  7.2 3.3 copy-start.4
  7.2 123.7 %reduce-scatter.4.cloned.1.call-start = ((), (), s32[]{:S(2)}) async-start(), calls=%async_computation.3 | async-start | bytes 4456448 | tf_op jit(solution)/shard_map/reduce_scatter | solution.py:40
  7.2 7.2 %collective-permute-start = (f32[64,1,1024]{2,0,1:T(8,128)}, f32[64,1,1024]{2,0,1:T(8,128)S(1)}, u32[]{:S(2)}, u32[]{:S(2)}) collective-permute-start(f32[64,1,1024]{2,0,1:T(8,128)} %bitcast.59), channel_id=1, source_target_pairs={{0,1},{1,2},{2,3},{3,4},{4,5},{5,6},{6,7},{7,0},{8,9},{9,10},{10,1... | collective-permute-start | bytes 786440 | tf_op jit(solution)/shard_map/ppermute | solution.py:18
  7.3 7.2 %collective-permute-start.1 = (f32[64,1,1024]{2,0,1:T(8,128)}, f32[64,1,1024]{2,0,1:T(8,128)S(1)}, u32[]{:S(2)}, u32[]{:S(2)}) collective-permute-start(f32[64,1,1024]{2,0,1:T(8,128)} %bitcast.60), channel_id=1, source_target_pairs={{0,7},{1,0},{2,1},{3,2},{4,3},{5,4},{6,5},{7,6},{8,15},{9,8},{10,9... | collective-permute-start | bytes 786440 | tf_op jit(solution)/shard_map/ppermute | solution.py:21
  14.5 7.0 %collective-permute-start.2 = (f32[64,1,1024]{2,0,1:T(8,128)S(1)}, f32[64,1,1024]{2,0,1:T(8,128)S(1)}, u32[]{:S(2)}, u32[]{:S(2)}) collective-permute-start(f32[64,1,1024]{2,0,1:T(8,128)S(1)} %collective-permute-done), channel_id=1, source_target_pairs={{0,1},{1,2},{2,3},{3,4},{4,5},{5,6},{6,7},{7,0},{8,9},{9,10},{10,1... | collective-permute-start | bytes 786440 | tf_op jit(solution)/shard_map/ppermute | solution.py:18
  14.5 7.0 %collective-permute-start.3 = (f32[64,1,1024]{2,0,1:T(8,128)S(1)}, f32[64,1,1024]{2,0,1:T(8,128)S(1)}, u32[]{:S(2)}, u32[]{:S(2)}) collective-permute-start(f32[64,1,1024]{2,0,1:T(8,128)S(1)} %collective-permute-done.1), channel_id=1, source_target_pairs={{0,7},{1,0},{2,1},{3,2},{4,3},{5,4},{6,5},{7,6},{8,15},{9,8},{10,9... | collective-permute-start | bytes 786440 | tf_op jit(solution)/shard_map/ppermute | solution.py:21
  21.5 7.0 %collective-permute-start.4 = (f32[64,1,1024]{2,0,1:T(8,128)S(1)}, f32[64,1,1024]{2,0,1:T(8,128)S(1)}, u32[]{:S(2)}, u32[]{:S(2)}) collective-permute-start(f32[64,1,1024]{2,0,1:T(8,128)S(1)} %collective-permute-done.2), channel_id=1, source_target_pairs={{0,1},{1,2},{2,3},{3,4},{4,5},{5,6},{6,7},{7,0},{8,9},{9,10},{10,1... | collective-permute-start | bytes 786440 | tf_op jit(solution)/shard_map/ppermute | solution.py:18
  21.5 7.0 %collective-permute-start.5 = (f32[64,1,1024]{2,0,1:T(8,128)S(1)}, f32[64,1,1024]{2,0,1:T(8,128)S(1)}, u32[]{:S(2)}, u32[]{:S(2)}) collective-permute-start(f32[64,1,1024]{2,0,1:T(8,128)S(1)} %collective-permute-done.3), channel_id=1, source_target_pairs={{0,7},{1,0},{2,1},{3,2},{4,3},{5,4},{6,5},{7,6},{8,15},{9,8},{10,9... | collective-permute-start | bytes 786440 | tf_op jit(solution)/shard_map/ppermute | solution.py:21
  28.5 7.0 %collective-permute-start.6 = (f32[64,1,1024]{2,0,1:T(8,128)S(1)}, f32[64,1,1024]{2,0,1:T(8,128)S(1)}, u32[]{:S(2)}, u32[]{:S(2)}) collective-permute-start(f32[64,1,1024]{2,0,1:T(8,128)S(1)} %collective-permute-done.4), channel_id=1, source_target_pairs={{0,1},{1,2},{2,3},{3,4},{4,5},{5,6},{6,7},{7,0},{8,9},{9,10},{10,1... | collective-permute-start | bytes 786440 | tf_op jit(solution)/shard_map/ppermute | solution.py:18
  52.9 78.1 %copy-start.7 = (s32[4,2]{0,1:T(2,128)S(1)}, s32[4,2]{0,1:T(2,128)}, u32[]{:S(2)}) copy-start(s32[4,2]{0,1:T(2,128)} %param.19) | copy-start | bytes 100
  52.9 78.2 %copy-start.8 = (s32[2,4]{1,0:T(2,128)S(1)}, s32[2,4]{1,0:T(2,128)}, u32[]{:S(2)}) copy-start(s32[2,4]{1,0:T(2,128)} %param.18) | copy-start | bytes 100
  52.9 104.7 %all-gather.5.cloned.1.call-start = ((), (), s32[]{:S(2)}) async-start(), calls=%async_computation.4 | async-start | bytes 2359296 | tf_op jit(solution)/shard_map/all_gather | solution.py:55
  130.9 80.2 %all-gather.7.cloned.1.call-start = ((), (), s32[]{:S(2)}) async-start(), calls=%async_computation.5 | async-start | bytes 2228224 | tf_op jit(solution)/shard_map/all_gather | solution.py:60
  162.2 4.9 copy-start.5
  165.3 119.5 %all-reduce.3.cloned.1.call-start = ((), (), s32[]{:S(2)}) async-start(), calls=%async_computation.6 | async-start | bytes 4194304 | tf_op jit(solution)/shard_map/psum | solution.py:64
  167.9 7.0 %collective-permute-start.7 = (f32[64,2,512]{2,0,1:T(8,128)S(1)}, f32[64,2,512]{2,0,1:T(8,128)S(1)}, u32[]{:S(2)}, u32[]{:S(2)}) collective-permute-start(f32[64,2,512]{2,0,1:T(8,128)S(1)} %get-tuple-element.14), channel_id=1, source_target_pairs={{0,1},{1,2},{2,3},{3,4},{4,5},{5,6},{6,7},{7,0},{8,9},{9,10},{10,1... | collective-permute-start | bytes 786440 | tf_op jit(solution)/shard_map/ppermute | solution.py:18
  168.2 50.1 %collective-permute-start.8 = (f32[64,2,512]{2,0,1:T(8,128)S(1)}, f32[64,2,512]{2,0,1:T(8,128)S(1)}, u32[]{:S(2)}, u32[]{:S(2)}) collective-permute-start(f32[64,2,512]{2,0,1:T(8,128)S(1)} %get-tuple-element.14), channel_id=1, source_target_pairs={{0,7},{1,0},{2,1},{3,2},{4,3},{5,4},{6,5},{7,6},{8,15},{9,8},{10,9... | collective-permute-start | bytes 786440 | tf_op jit(solution)/shard_map/ppermute | solution.py:21
  174.9 44.4 %collective-permute-start.9 = (f32[64,2,512]{2,0,1:T(8,128)S(1)}, f32[64,2,512]{2,0,1:T(8,128)S(1)}, u32[]{:S(2)}, u32[]{:S(2)}) collective-permute-start(f32[64,2,512]{2,0,1:T(8,128)S(1)} %collective-permute-done.7), channel_id=1, source_target_pairs={{0,1},{1,2},{2,3},{3,4},{4,5},{5,6},{6,7},{7,0},{8,9},{9,10},{10,1... | collective-permute-start | bytes 786440 | tf_op jit(solution)/shard_map/ppermute | solution.py:18
  218.2 156.4 %reduce-scatter.6.cloned.1.call-start = ((), (), s32[]{:S(2)}) async-start(), calls=%async_computation.7 | async-start | bytes 4456448 | tf_op jit(solution)/shard_map/reduce_scatter | solution.py:40
  218.2 5.0 collective-permute-start.10
  219.3 7.7 %collective-permute-start.11 = (f32[64,2,512]{2,0,1:T(8,128)S(1)}, f32[64,2,512]{2,0,1:T(8,128)S(1)}, u32[]{:S(2)}, u32[]{:S(2)}) collective-permute-start(f32[64,2,512]{2,0,1:T(8,128)S(1)} %collective-permute-done.9), channel_id=1, source_target_pairs={{0,1},{1,2},{2,3},{3,4},{4,5},{5,6},{6,7},{7,0},{8,9},{9,10},{10,1... | collective-permute-start | bytes 786440 | tf_op jit(solution)/shard_map/ppermute | solution.py:18
  223.2 7.0 %collective-permute-start.12 = (f32[64,2,512]{2,0,1:T(8,128)S(1)}, f32[64,2,512]{2,0,1:T(8,128)S(1)}, u32[]{:S(2)}, u32[]{:S(2)}) collective-permute-start(f32[64,2,512]{2,0,1:T(8,128)S(1)} %collective-permute-done.10), channel_id=1, source_target_pairs={{0,7},{1,0},{2,1},{3,2},{4,3},{5,4},{6,5},{7,6},{8,15},{9,8},{10,9... | collective-permute-start | bytes 786440 | tf_op jit(solution)/shard_map/ppermute | solution.py:21
  227.0 7.9 %collective-permute-start.13 = (f32[64,2,512]{2,0,1:T(8,128)S(1)}, f32[64,2,512]{2,0,1:T(8,128)S(1)}, u32[]{:S(2)}, u32[]{:S(2)}) collective-permute-start(f32[64,2,512]{2,0,1:T(8,128)S(1)} %collective-permute-done.11), channel_id=1, source_target_pairs={{0,1},{1,2},{2,3},{3,4},{4,5},{5,6},{6,7},{7,0},{8,9},{9,10},{10,1... | collective-permute-start | bytes 786440 | tf_op jit(solution)/shard_map/ppermute | solution.py:18
  297.0 103.4 %all-gather.9.cloned.1.call-start = ((), (), s32[]{:S(2)}) async-start(), calls=%async_computation.8 | async-start | bytes 2359296 | tf_op jit(solution)/shard_map/all_gather | solution.py:55
  374.6 89.3 %all-gather.11.cloned.1.call-start = ((), (), s32[]{:S(2)}) async-start(), calls=%async_computation.9 | async-start | bytes 2228224 | tf_op jit(solution)/shard_map/all_gather | solution.py:60
  409.0 3.0 copy-start.1
  414.4 49.5 %copy-start.2 = (f32[4,256,256]{2,1,0:T(8,128)S(1)}, f32[4,256,256]{2,1,0:T(8,128)}, u32[]{:S(2)}) copy-start(f32[4,256,256]{2,1,0:T(8,128)} %param.17) | copy-start | bytes 3145732
  417.4 2.4 copy-start.6
  418.1 117.3 %all-reduce.5.cloned.1.call-start = ((), (), s32[]{:S(2)}) async-start(), calls=%async_computation.10 | async-start | bytes 4194304 | tf_op jit(solution)/shard_map/psum | solution.py:64
  420.6 7.3 %collective-permute-start.14 = (f32[64,4,256]{2,0,1:T(8,128)}, f32[64,4,256]{2,0,1:T(8,128)}, u32[]{:S(2)}, u32[]{:S(2)}) collective-permute-start(f32[64,4,256]{2,0,1:T(8,128)} %get-tuple-element.12), channel_id=1, source_target_pairs={{0,1},{1,2},{2,3},{3,4},{4,5},{5,6},{6,7},{7,0},{8,9},{9,10},{10,1... | collective-permute-start | bytes 786440 | tf_op jit(solution)/shard_map/ppermute | solution.py:18
  420.9 48.0 %collective-permute-start.15 = (f32[64,4,256]{2,0,1:T(8,128)}, f32[64,4,256]{2,0,1:T(8,128)}, u32[]{:S(2)}, u32[]{:S(2)}) collective-permute-start(f32[64,4,256]{2,0,1:T(8,128)} %get-tuple-element.12), channel_id=1, source_target_pairs={{0,7},{1,0},{2,1},{3,2},{4,3},{5,4},{6,5},{7,6},{8,15},{9,8},{10,9... | collective-permute-start | bytes 786440 | tf_op jit(solution)/shard_map/ppermute | solution.py:21
  427.9 42.1 %collective-permute-start.16 = (f32[64,4,256]{2,0,1:T(8,128)}, f32[64,4,256]{2,0,1:T(8,128)S(1)}, u32[]{:S(2)}, u32[]{:S(2)}) collective-permute-start(f32[64,4,256]{2,0,1:T(8,128)} %collective-permute-done.14), channel_id=1, source_target_pairs={{0,1},{1,2},{2,3},{3,4},{4,5},{5,6},{6,7},{7,0},{8,9},{9,10},{10,1... | collective-permute-start | bytes 786440 | tf_op jit(solution)/shard_map/ppermute | solution.py:18
  468.8 152.1 %reduce-scatter.8.cloned.1.call-start = ((), (), s32[]{:S(2)}) async-start(), calls=%async_computation.11 | async-start | bytes 4456448 | tf_op jit(solution)/shard_map/reduce_scatter | solution.py:40
  468.9 5.3 collective-permute-start.17
  470.0 8.0 %collective-permute-start.18 = (f32[64,4,256]{2,0,1:T(8,128)S(1)}, f32[64,4,256]{2,0,1:T(8,128)S(1)}, u32[]{:S(2)}, u32[]{:S(2)}) collective-permute-start(f32[64,4,256]{2,0,1:T(8,128)S(1)} %collective-permute-done.16), channel_id=1, source_target_pairs={{0,1},{1,2},{2,3},{3,4},{4,5},{5,6},{6,7},{7,0},{8,9},{9,10},{10,1... | collective-permute-start | bytes 786440 | tf_op jit(solution)/shard_map/ppermute | solution.py:18
  474.2 6.9 %collective-permute-start.19 = (f32[64,4,256]{2,0,1:T(8,128)S(1)}, f32[64,4,256]{2,0,1:T(8,128)S(1)}, u32[]{:S(2)}, u32[]{:S(2)}) collective-permute-start(f32[64,4,256]{2,0,1:T(8,128)S(1)} %collective-permute-done.17), channel_id=1, source_target_pairs={{0,7},{1,0},{2,1},{3,2},{4,3},{5,4},{6,5},{7,6},{8,15},{9,8},{10,9... | collective-permute-start | bytes 786440 | tf_op jit(solution)/shard_map/ppermute | solution.py:21
  477.9 7.7 %collective-permute-start.20 = (f32[64,4,256]{2,0,1:T(8,128)S(1)}, f32[64,4,256]{2,0,1:T(8,128)S(1)}, u32[]{:S(2)}, u32[]{:S(2)}) collective-permute-start(f32[64,4,256]{2,0,1:T(8,128)S(1)} %collective-permute-done.18), channel_id=1, source_target_pairs={{0,1},{1,2},{2,3},{3,4},{4,5},{5,6},{6,7},{7,0},{8,9},{9,10},{10,1... | collective-permute-start | bytes 786440 | tf_op jit(solution)/shard_map/ppermute | solution.py:18
  543.2 0.9 copy-start.3
Sparse Core Ops, SparseCore 0:
  53.0 77.7 reduce-scatter.3
  133.2 24.3 all-gather.4
  165.4 45.5 all-gather.6
  218.3 66.4 all-reduce.2
  297.1 77.3 reduce-scatter.5
  376.1 24.3 all-gather.8
  418.2 45.5 all-gather.10
  469.0 66.4 all-reduce.4
  543.4 77.4 reduce-scatter.7
